TPU v7x, 256 devices: a whole 4x4x8 slice. The times are simulated.
256 devices in a mesh: space: 16 (over z_lo, y), view: 16 (over x, z_hi, core).
Axes of the slice: x: 4, y: 4, z: 8 (z_hi: 2, z_lo: 4; z = z_hi * 4 + z_lo), core: 2. Of those that a mesh axis runs over, the one named last changes fastest.
Arguments:
- estimate: float32 [16, 64, 4096], P('space', None, 'view'), may hold values from 0.5 to 2
- measured: float32 [16, 16, 64, 4096], P('view', 'space'), may hold values from 0.2 to 5
- kernel_x: float32 [16, 7], P('view'), may hold values from 0.2 to 1
- kernel_y: float32 [16, 7], P('view'), may hold values from 0.2 to 1
- kernel_z: float32 [16, 15], P('view'), may hold values from 0.2 to 1
- neighbors: int32 [16, 6], P('space'), may hold values from -1 to 15, as said below
- inside: int32 [16], P('space'), may hold values 0 or 1
Outputs:
- deconvolved: float32 [16, 64, 4096], P('space', None, 'view')
Inputs may be any that keep to these rules, and one draw needn't show every extreme that they name: neighbors[b, f] is the brick across face f of brick b (faces in order: low and high along the first, second and third cell dimension), or -1 at the window's border; if neighbors[b, f] = c then neighbors[c, f + 1 - 2 (f % 2)] = b; the window is a box of 2 x 2 x (4) bricks, and the 1 bricks of one index of space lie in a row along the third dimension.
All inputs are finite; a program needn't handle non-finite values. No bound on the sum of `inside` on one device may be relied on, other than what follows from the above.
Results may differ from a plain program's by a relative error of at most 0.0001.
Values sent between devices are 32-bit elements; how exact they have to be, the bound alone decides.
No kernel may reach another device: no remote copies, remote signals or barrier semaphores. Data moves between devices by JAX's collectives and lax.ppermute only.
A program may use at most 128 MiB of HBM per device.

v0:
```python
import jax
import jax.numpy as jnp
from jax import lax
from jax.sharding import PartitionSpec as P

ITERS = 2


def normalized(kernel):
    return kernel / jnp.sum(kernel)


def edge_planes(volume, axis_dim, radius):
    length = volume.shape[axis_dim]
    first_part = lax.slice_in_dim(volume, 0, radius, axis=axis_dim)
    last_part = lax.slice_in_dim(volume, length - radius, length, axis=axis_dim)
    stacked = jnp.stack([first_part, last_part], axis=1)
    return jnp.moveaxis(stacked, axis_dim + 1, 2)


def pick_faces(neighbors, axis_dim):
    low_ids = neighbors[:, 2 * axis_dim - 2]
    high_ids = neighbors[:, 2 * axis_dim - 1]

    def fold_faces(running, incoming, first_row):
        count_rows = incoming.shape[0]
        brick_ids = jnp.arange(count_rows, dtype=jnp.int32)
        low_pick = (low_ids[:, None] == brick_ids[None, :]).astype(jnp.float32)
        high_pick = (high_ids[:, None] == brick_ids[None, :]).astype(jnp.float32)
        low_part = jnp.einsum(
            "br,rpac->bpac", low_pick, incoming[:, 1], precision=lax.Precision.HIGHEST
        )
        high_part = jnp.einsum(
            "br,rpac->bpac", high_pick, incoming[:, 0], precision=lax.Precision.HIGHEST
        )
        return jnp.stack([low_part, high_part], axis=1)

    return fold_faces


def with_halo(volume, neighbors, axis_dim, radius, source):
    edge_slabs = edge_planes(volume, axis_dim, radius)
    zeros_halo = jnp.zeros_like(edge_slabs)
    fold_faces = pick_faces(neighbors, axis_dim)
    if source == "estimate":
        halo_faces = fold_faces(
            zeros_halo, lax.all_gather(edge_slabs, "space", axis=0, tiled=True), jnp.int32(0)
        )
    elif source == "blurred":
        halo_faces = fold_faces(
            zeros_halo, lax.all_gather(edge_slabs, "space", axis=0, tiled=True), jnp.int32(0)
        )
    elif source == "blurred_z":
        halo_faces = fold_faces(
            zeros_halo, lax.all_gather(edge_slabs, "space", axis=0, tiled=True), jnp.int32(0)
        )
    elif source == "ratio_z":
        halo_faces = fold_faces(
            zeros_halo, lax.all_gather(edge_slabs, "space", axis=0, tiled=True), jnp.int32(0)
        )
    else:
        halo_faces = fold_faces(
            zeros_halo, lax.all_gather(edge_slabs, "space", axis=0, tiled=True), jnp.int32(0)
        )
    halo_faces = jnp.moveaxis(halo_faces, 2, axis_dim + 1)
    return jnp.concatenate([halo_faces[:, 0], volume, halo_faces[:, 1]], axis=axis_dim)


def convolve(extended, kernel, axis_dim, flipped):
    radius = (kernel.shape[0] - 1) // 2
    length = extended.shape[axis_dim] - 2 * radius
    out_shape = list(extended.shape)
    out_shape[axis_dim] = length
    summed = jnp.zeros(tuple(out_shape), jnp.float32)
    for position in range(2 * radius + 1):
        weight = kernel[2 * radius - position] if flipped else kernel[position]
        summed = summed + weight * lax.slice_in_dim(
            extended, position, position + length, axis=axis_dim
        )
    return summed


def shards(estimate, measured, kernel_x, kernel_y, kernel_z, neighbors, inside):
    brick_side = estimate.shape[1]
    share_cells = estimate.reshape(
        estimate.shape[0], brick_side, estimate.shape[2] // brick_side, brick_side
    )
    recorded_all = measured.reshape(
        measured.shape[0], measured.shape[1], brick_side, brick_side, brick_side
    )
    share_rows = share_cells.shape[2]
    row_start = lax.axis_index("view") * share_rows
    view_count = recorded_all.shape[0] * lax.axis_size("view")
    radius_x = (kernel_x.shape[1] - 1) // 2
    radius_y = (kernel_y.shape[1] - 1) // 2
    radius_z = (kernel_z.shape[1] - 1) // 2
    keep_mask = (inside > 0)[:, None, None, None]
    share_now = share_cells
    full_now = None
    for sweep_no in range(ITERS):
        if full_now is None:
            full_now = lax.all_gather(share_now, "view", axis=2, tiled=True)
            extended = with_halo(full_now, neighbors, 1, radius_x, "estimate")
        else:
            extended = with_halo(full_now, neighbors, 1, radius_x, "estimate")
        along_x = normalized(kernel_x[0])
        along_y = normalized(kernel_y[0])
        along_z = normalized(kernel_z[0])
        blurred = convolve(extended, along_x, 1, False)
        blurred = convolve(with_halo(blurred, neighbors, 2, radius_y, "blurred"), along_y, 2, False)
        blurred = convolve(
            with_halo(blurred, neighbors, 3, radius_z, "blurred_z"), along_z, 3, False
        )
        quotient = recorded_all[0] / blurred
        spread = convolve(with_halo(quotient, neighbors, 3, radius_z, "ratio_z"), along_z, 3, True)
        spread = convolve(with_halo(spread, neighbors, 2, radius_y, "ratio"), along_y, 2, True)
        spread = convolve(with_halo(spread, neighbors, 1, radius_x, "ratio"), along_x, 1, True)
        final_sweep = sweep_no == ITERS - 1
        if not final_sweep:
            summed = lax.psum(spread, "view")
            full_now = full_now * jnp.where(keep_mask, summed / view_count, 1.0)
        else:
            summed = lax.psum_scatter(spread, "view", scatter_dimension=2, tiled=True)
            own_rows = lax.dynamic_slice_in_dim(full_now, row_start, share_rows, 2)
            share_now = own_rows * jnp.where(keep_mask, summed / view_count, 1.0)
            full_now = None
    return share_now.reshape(share_now.shape[0], brick_side, share_rows * brick_side)


def solution(mesh):
    placed = (
        P("space", None, "view"),
        P("view", "space", None, None),
        P("view", None),
        P("view", None),
        P("view", None),
        P("space", None),
        P("space"),
    )
    return jax.shard_map(
        shards, mesh=mesh, in_specs=placed, out_specs=P("space", None, "view"), check_vma=False
    )
```

profile of v0, /device:TPU:8, one launch (start us, length us, event | category | flops | bytes accessed | tf_op | source)
XLA Modules:
  0.0 1770.8 jit_solution(11116695997213249861)
XLA Ops:
  8.3 67.6 %all-gather.14.cloned.1.call-done = f32[1,64,64,64]{3,1,0,2:T(8,128)} async-done(((f32[1,64,4,64]{3,1,0,2:T(8,128)}), f32[1,64,64,64]{3,1,0,2:T(8,128)}) %all-gather.14.cloned.1.call-update) | async-done | bytes 1048592 | tf_op jit(solution)/shard_map/all_gather | solution.py:102
  84.2 75.9 %all-gather.16.cloned.1.call-done = f32[16,2,3,64,64]{4,3,2,1,0:T(8,128)} async-done(((f32[1,2,3,64,64]{4,3,2,1,0:T(8,128)}), f32[16,2,3,64,64]{4,3,2,1,0:T(8,128)}) %all-gather.16.cloned.1.call-update) | async-done | bytes 1572880 | tf_op jit(solution)/shard_map/all_gather | solution.py:47
  177.2 82.1 %all-gather.18.cloned.1.call-done = f32[16,2,3,64,64]{4,3,2,1,0:T(8,128)} async-done(((f32[1,2,3,64,64]{4,3,2,1,0:T(8,128)}), f32[16,2,3,64,64]{4,3,2,1,0:T(8,128)}) %all-gather.18.cloned.1.call-update) | async-done | bytes 1572880 | tf_op jit(solution)/shard_map/all_gather | solution.py:51
  266.0 6.6 fusion.117
  287.2 88.8 %all-gather.20.cloned.1.call-done = f32[16,2,7,64,64]{4,3,2,1,0:T(8,128)} async-done(((f32[1,2,7,64,64]{4,3,2,1,0:T(8,128)}), f32[16,2,7,64,64]{4,3,2,1,0:T(8,128)}) %all-gather.20.cloned.1.call-update) | async-done | bytes 3670032 | tf_op jit(solution)/shard_map/all_gather | solution.py:55
  395.0 24.2 %fusion.239 = f32[1,64,64,64]{3,2,1,0:T(8,128)S(1)} fusion(f32[1,64,64,64]{3,2,1,0:T(8,128)S(1)} %copy-done.4, f32[1,64,64,7]{3,2,1,0:T(8,128)S(1)} %get-tuple-element.20, f32[1,64,64,64]{3,2,1,0:T(8,128)S(1)} %fusion.117, f32[1,64,64,7]{3,2,1,0:T(8,128)S(1)} %get-tuple-element.19, f32[]{:T(128)} %bitcast.96, f32[]{:T(128)} %bitcast.95, f32[]{:T(128)} %bitcast.94, ...), kind=kLoop, calls=%fused_computation.402 | loop fusion | flops 11534336 | bytes 3375164 | tf_op jit(solution)/shard_map/div | solution.py:114
  425.6 93.2 %all-gather.22.cloned.1.call-done = f32[16,2,7,64,64]{4,3,2,1,0:T(8,128)} async-done(((f32[1,2,7,64,64]{4,3,2,1,0:T(8,128)}), f32[16,2,7,64,64]{4,3,2,1,0:T(8,128)}) %all-gather.22.cloned.1.call-update) | async-done | bytes 3670032 | tf_op jit(solution)/shard_map/all_gather | solution.py:59
  539.5 36.4 %fusion.206 = f32[1,64,64,64]{3,2,1,0:T(8,128)} fusion(f32[1,64,64,7]{3,2,1,0:T(8,128)} %get-tuple-element.18, f32[1,64,64,64]{3,2,1,0:T(8,128)S(1)} %copy-done.3, f32[1,64,64,7]{3,2,1,0:T(8,128)} %get-tuple-element.17, f32[]{:T(128)} %bitcast.96, f32[]{:T(128)} %bitcast.95, f32[]{:T(128)} %bitcast.94, f32[]{:T(128)} %bitcast.93, f32[]{:T(128)} %bitcast.92, ...), kind=kLoop, calls=%fused_computation.343 | loop fusion | flops 11272192 | bytes 2326588 | tf_op jit(solution)/shard_map/add | solution.py:77
  577.8 84.3 %all-gather.24.cloned.1.call-done = f32[16,2,3,64,64]{4,3,2,1,0:T(8,128)} async-done(((f32[1,2,3,64,64]{4,3,2,1,0:T(8,128)}), f32[16,2,3,64,64]{4,3,2,1,0:T(8,128)}) %all-gather.24.cloned.1.call-update) | async-done | bytes 1572880 | tf_op jit(solution)/shard_map/all_gather | solution.py:63
  668.8 7.1 fusion.103
  676.7 84.3 %all-gather.26.cloned.1.call-done = f32[16,2,3,64,64]{4,3,2,1,0:T(8,128)} async-done(((f32[1,2,3,64,64]{4,3,2,1,0:T(8,128)}), f32[16,2,3,64,64]{4,3,2,1,0:T(8,128)}) %all-gather.26.cloned.1.call-update) | async-done | bytes 1572880 | tf_op jit(solution)/shard_map/all_gather | solution.py:63
  767.3 7.5 fusion.47
  775.6 199.1 %all-reduce.2.cloned.1.call-done = f32[1,64,64,64]{3,2,1,0:T(8,128)} async-done(((f32[1,64,64,64]{3,2,1,0:T(8,128)}), f32[1,64,64,64]{3,2,1,0:T(8,128)}) %all-reduce.2.cloned.1.call-update) | async-done | bytes 1048592 | tf_op jit(solution)/shard_map/psum | solution.py:120
  979.2 82.8 %all-gather.28.cloned.1.call-done = f32[16,2,3,64,64]{4,3,2,1,0:T(8,128)} async-done(((f32[1,2,3,64,64]{4,3,2,1,0:T(8,128)}), f32[16,2,3,64,64]{4,3,2,1,0:T(8,128)}) %all-gather.28.cloned.1.call-update) | async-done | bytes 1572880 | tf_op jit(solution)/shard_map/all_gather | solution.py:47
  1077.0 84.1 %all-gather.30.cloned.1.call-done = f32[16,2,3,64,64]{4,3,2,1,0:T(8,128)} async-done(((f32[1,2,3,64,64]{4,3,2,1,0:T(8,128)}), f32[16,2,3,64,64]{4,3,2,1,0:T(8,128)}) %all-gather.30.cloned.1.call-update) | async-done | bytes 1572880 | tf_op jit(solution)/shard_map/all_gather | solution.py:51
  1167.9 6.6 fusion.89
  1181.0 93.1 %all-gather.32.cloned.1.call-done = f32[16,2,7,64,64]{4,3,2,1,0:T(8,128)} async-done(((f32[1,2,7,64,64]{4,3,2,1,0:T(8,128)}), f32[16,2,7,64,64]{4,3,2,1,0:T(8,128)}) %all-gather.32.cloned.1.call-update) | async-done | bytes 3670032 | tf_op jit(solution)/shard_map/all_gather | solution.py:55
  1293.3 24.2 %fusion.166 = f32[1,64,64,64]{3,2,1,0:T(8,128)S(1)} fusion(f32[1,64,64,64]{3,2,1,0:T(8,128)S(1)} %copy-done.5, f32[1,64,64,7]{3,2,1,0:T(8,128)S(1)} %get-tuple-element.16, f32[1,64,64,64]{3,2,1,0:T(8,128)S(1)} %copy-done.1, f32[1,64,64,7]{3,2,1,0:T(8,128)S(1)} %get-tuple-element.15, f32[]{:T(128)} %bitcast.96, f32[]{:T(128)} %bitcast.95, f32[]{:T(128)} %bitcast.94, ...), kind=kLoop, calls=%fused_computation.269 | loop fusion | flops 11534336 | bytes 3375164 | tf_op jit(solution)/shard_map/div | solution.py:114
  1326.3 92.9 %all-gather.34.cloned.1.call-done = f32[16,2,7,64,64]{4,3,2,1,0:T(8,128)} async-done(((f32[1,2,7,64,64]{4,3,2,1,0:T(8,128)}), f32[16,2,7,64,64]{4,3,2,1,0:T(8,128)}) %all-gather.34.cloned.1.call-update) | async-done | bytes 3670032 | tf_op jit(solution)/shard_map/all_gather | solution.py:59
  1439.7 36.2 %fusion.133 = f32[1,64,64,64]{3,2,1,0:T(8,128)} fusion(f32[1,64,64,7]{3,2,1,0:T(8,128)} %get-tuple-element.14, f32[1,64,64,64]{3,2,1,0:T(8,128)S(1)} %fusion.166, f32[1,64,64,7]{3,2,1,0:T(8,128)} %get-tuple-element.13, f32[]{:T(128)} %bitcast.96, f32[]{:T(128)} %bitcast.95, f32[]{:T(128)} %bitcast.94, f32[]{:T(128)} %bitcast.93, f32[]{:T(128)} %bitcast.92, ...), kind=kLoop, calls=%fused_computation.210 | loop fusion | flops 11272192 | bytes 2326588 | tf_op jit(solution)/shard_map/add | solution.py:77
  1477.8 84.3 %all-gather.36.cloned.1.call-done = f32[16,2,3,64,64]{4,3,2,1,0:T(8,128)} async-done(((f32[1,2,3,64,64]{4,3,2,1,0:T(8,128)}), f32[16,2,3,64,64]{4,3,2,1,0:T(8,128)}) %all-gather.36.cloned.1.call-update) | async-done | bytes 1572880 | tf_op jit(solution)/shard_map/all_gather | solution.py:63
  1568.9 6.9 fusion.75
  1576.5 84.3 %all-gather.38.cloned.1.call-done = f32[16,2,3,64,64]{4,3,2,1,0:T(8,128)} async-done(((f32[1,2,3,64,64]{4,3,2,1,0:T(8,128)}), f32[16,2,3,64,64]{4,3,2,1,0:T(8,128)}) %all-gather.38.cloned.1.call-update) | async-done | bytes 1572880 | tf_op jit(solution)/shard_map/all_gather | solution.py:63
  1676.1 86.1 %reduce-scatter.2.cloned.1.call-done = f32[1,64,4,64]{3,1,0,2:T(8,128)} async-done(((f32[1,64,64,64]{3,1,0,2:T(8,128)}), f32[1,64,4,64]{3,1,0,2:T(8,128)}) %reduce-scatter.2.cloned.1.call-update) | async-done | bytes 65552 | tf_op jit(solution)/shard_map/reduce_scatter | solution.py:123
  (188 shorter events, 216.8 us)
Async XLA Ops:
  6.5 72.1 %copy-start.15 = (f32[1,7]{1,0:T(1,128)S(1)}, f32[1,7]{1,0:T(1,128)}, u32[]{:S(2)}) copy-start(f32[1,7]{1,0:T(1,128)} %param.9) | copy-start | bytes 88
  6.5 72.8 %copy-start.14 = (s32[1,6]{1,0:T(1,128)S(1)}, s32[1,6]{1,0:T(1,128)}, u32[]{:S(2)}) copy-start(s32[1,6]{1,0:T(1,128)} %param.12) | copy-start | bytes 76
  6.5 69.3 %all-gather.14.cloned.1.call-start = ((), (), s32[]{:S(2)}) async-start(), calls=%async_computation.1 | async-start | bytes 2228224 | tf_op jit(solution)/shard_map/all_gather | solution.py:102
  8.2 151.9 %all-gather.16.cloned.1.call-start = ((), (), s32[]{:S(2)}) async-start(), calls=%async_computation.2 | async-start | bytes 3342336 | tf_op jit(solution)/shard_map/all_gather | solution.py:47
  78.6 180.7 %all-gather.18.cloned.1.call-start = ((), (), s32[]{:S(2)}) async-start(), calls=%async_computation.3 | async-start | bytes 3342336 | tf_op jit(solution)/shard_map/all_gather | solution.py:51
  166.4 8.9 copy-start.16
  174.9 201.1 %all-gather.20.cloned.1.call-start = ((), (), s32[]{:S(2)}) async-start(), calls=%async_computation.4 | async-start | bytes 7798784 | tf_op jit(solution)/shard_map/all_gather | solution.py:55
  277.7 5.3 copy-start.17
  277.7 5.9 copy-start.13
  282.6 236.2 %all-gather.22.cloned.1.call-start = ((), (), s32[]{:S(2)}) async-start(), calls=%async_computation.5 | async-start | bytes 7798784 | tf_op jit(solution)/shard_map/all_gather | solution.py:59
  425.4 236.7 %all-gather.24.cloned.1.call-start = ((), (), s32[]{:S(2)}) async-start(), calls=%async_computation.6 | async-start | bytes 3342336 | tf_op jit(solution)/shard_map/all_gather | solution.py:63
  534.5 5.0 copy-start.3
  577.7 183.3 %all-gather.26.cloned.1.call-start = ((), (), s32[]{:S(2)}) async-start(), calls=%async_computation.7 | async-start | bytes 3342336 | tf_op jit(solution)/shard_map/all_gather | solution.py:63
  664.2 4.6 copy-start.8
  676.6 298.1 %all-reduce.2.cloned.1.call-start = ((), (), s32[]{:S(2)}) async-start(), calls=%async_computation.8 | async-start | bytes 4194304 | tf_op jit(solution)/shard_map/psum | solution.py:120
  774.9 287.1 %all-gather.28.cloned.1.call-start = ((), (), s32[]{:S(2)}) async-start(), calls=%async_computation.9 | async-start | bytes 3342336 | tf_op jit(solution)/shard_map/all_gather | solution.py:47
  978.3 90.0 %copy-start.6 = (f32[1,64,64,64]{3,2,1,0:T(8,128)}, f32[1,64,64,64]{3,2,1,0:T(8,128)S(1)}, u32[]{:S(2)}) copy-start(f32[1,64,64,64]{3,2,1,0:T(8,128)S(1)} %select_multiply_fusion) | copy-start | bytes 3145732
  979.1 182.1 %all-gather.30.cloned.1.call-start = ((), (), s32[]{:S(2)}) async-start(), calls=%async_computation.10 | async-start | bytes 3342336 | tf_op jit(solution)/shard_map/all_gather | solution.py:51
  1076.8 197.3 %all-gather.32.cloned.1.call-start = ((), (), s32[]{:S(2)}) async-start(), calls=%async_computation.11 | async-start | bytes 7798784 | tf_op jit(solution)/shard_map/all_gather | solution.py:55
  1163.3 4.6 copy-start.12
  1180.7 238.4 %all-gather.34.cloned.1.call-start = ((), (), s32[]{:S(2)}) async-start(), calls=%async_computation.12 | async-start | bytes 7798784 | tf_op jit(solution)/shard_map/all_gather | solution.py:59
  1325.8 236.4 %all-gather.36.cloned.1.call-start = ((), (), s32[]{:S(2)}) async-start(), calls=%async_computation.13 | async-start | bytes 3342336 | tf_op jit(solution)/shard_map/all_gather | solution.py:63
  1477.8 183.1 %all-gather.38.cloned.1.call-start = ((), (), s32[]{:S(2)}) async-start(), calls=%async_computation.14 | async-start | bytes 3342336 | tf_op jit(solution)/shard_map/all_gather | solution.py:63
  1576.5 185.7 %reduce-scatter.2.cloned.1.call-start = ((), (), s32[]{:S(2)}) async-start(), calls=%async_computation.15 | async-start | bytes 2228224 | tf_op jit(solution)/shard_map/reduce_scatter | solution.py:123
  (9 other events, 25.6 us)
Sparse Core Ops, SparseCore 0:
  10.0 65.7 all-gather.13
  78.7 81.3 all-gather.15
  175.0 84.2 all-gather.17
  282.7 93.2 all-gather.19
  425.5 93.2 all-gather.21
  577.9 84.2 all-gather.23
  676.8 84.2 all-gather.25
  775.0 199.6 all-reduce.1
  979.2 82.7 all-gather.27
  1076.9 84.2 all-gather.29
  1180.9 93.2 all-gather.31
  1325.9 93.2 all-gather.33
  1477.9 84.2 all-gather.35
  1576.6 84.2 all-gather.37
  1676.2 85.9 reduce-scatter.1
where the time goes:
time: 1780 us; the launch traced here: 1770 us
  waiting for transfers between devices  1380 us (78%)
  other arithmetic  190 us (11%)
  local copies, waits for them, and re-layouts  114 us (6%)
  matrix products  66 us (4%)
    all_gather x12, waiting for transfers between devices, with_halo(): lax.all_gather(edge_slabs, 'space', axis=0, tiled=True)  1030 us
    psum x1, waiting for transfers between devices, shards(): summed = lax.psum(spread, 'view')  199 us
    add x10, other arithmetic, convolve(): summed + weight * lax.slice_in_dim(extended, position, position + length,...  126 us
    reduce_scatter x1, waiting for transfers between devices, shards(): summed = lax.psum_scatter(spread, 'view', scatter_dimension=2, tiled=True)  86.1 us
    all_gather x1, waiting for transfers between devices, shards(): full_now = lax.all_gather(share_now, 'view', axis=2, tiled=True)  67.6 us
    div x2, other arithmetic, shards(): quotient = recorded_all[0] / blurred  48.4 us
  transfers between devices with their start and end apart: 15, of which 15 were waited for; matrix products, arithmetic and copies ran while one was open for 1% of the time, Pallas kernels for 0%

commit v1 on v0

--- a/solution.py
+++ b/solution.py
@@ -4,6 +4,11 @@
 from jax.sharding import PartitionSpec as P
 
 ITERS = 2
+
+
+def add_all(x, axis):
+    parts = lax.all_gather(x, axis)
+    return jnp.sum(parts, axis=0)
 
 
 def normalized(kernel):
@@ -117,7 +122,7 @@
         spread = convolve(with_halo(spread, neighbors, 1, radius_x, "ratio"), along_x, 1, True)
         final_sweep = sweep_no == ITERS - 1
         if not final_sweep:
-            summed = lax.psum(spread, "view")
+            summed = add_all(spread, "view")
             full_now = full_now * jnp.where(keep_mask, summed / view_count, 1.0)
         else:
             summed = lax.psum_scatter(spread, "view", scatter_dimension=2, tiled=True)

time: 1780 us -> 1900 us (1.067)
  waiting for transfers between devices: 1380 us -> 1490 us
    all_gather x0 -> x1, waiting for transfers between devices: none -> 307 us  [add_all(): parts = lax.all_gather(x, axis)]
    psum x1 -> x0, waiting for transfers between devices: 199 us -> none  [shards(): summed = lax.psum(spread, 'view')]
where the time goes in v1:
time: 1900 us; the launch traced here: 1890 us
  waiting for transfers between devices  1490 us (78%)
  other arithmetic  207 us (11%)
  local copies, waits for them, and re-layouts  114 us (6%)
  matrix products  67.1 us (4%)
    all_gather x12, waiting for transfers between devices, with_halo(): lax.all_gather(edge_slabs, 'space', axis=0, tiled=True)  1030 us
    all_gather x1, waiting for transfers between devices, add_all(): parts = lax.all_gather(x, axis)  307 us
    add x10, other arithmetic, convolve(): summed + weight * lax.slice_in_dim(extended, position, position + length,...  128 us
    reduce_scatter x1, waiting for transfers between devices, shards(): summed = lax.psum_scatter(spread, 'view', scatter_dimension=2, tiled=True)  86.1 us
    all_gather x1, waiting for transfers between devices, shards(): full_now = lax.all_gather(share_now, 'view', axis=2, tiled=True)  67.6 us
    div x2, other arithmetic, shards(): quotient = recorded_all[0] / blurred  48.8 us
  transfers between devices with their start and end apart: 15, of which 15 were waited for; matrix products, arithmetic and copies ran while one was open for 1% of the time, Pallas kernels for 0%

profile of v1, /device:TPU:8, one launch (start us, length us, event | category | flops | bytes accessed | tf_op | source)
XLA Modules:
  0.0 1893.3 jit_solution(8635521364183669051)
XLA Ops:
  8.3 67.6 %all-gather.16.cloned.1.call-done = f32[1,64,64,64]{3,1,0,2:T(8,128)} async-done(((f32[1,64,4,64]{3,1,0,2:T(8,128)}), f32[1,64,64,64]{3,1,0,2:T(8,128)}) %all-gather.16.cloned.1.call-update) | async-done | bytes 1048592 | tf_op jit(solution)/shard_map/all_gather | solution.py:107
  84.1 76.0 %all-gather.18.cloned.1.call-done = f32[16,2,3,64,64]{4,3,2,1,0:T(8,128)} async-done(((f32[1,2,3,64,64]{4,3,2,1,0:T(8,128)}), f32[16,2,3,64,64]{4,3,2,1,0:T(8,128)}) %all-gather.18.cloned.1.call-update) | async-done | bytes 1572880 | tf_op jit(solution)/shard_map/all_gather | solution.py:52
  177.3 82.0 %all-gather.20.cloned.1.call-done = f32[16,2,3,64,64]{4,3,2,1,0:T(8,128)} async-done(((f32[1,2,3,64,64]{4,3,2,1,0:T(8,128)}), f32[16,2,3,64,64]{4,3,2,1,0:T(8,128)}) %all-gather.20.cloned.1.call-update) | async-done | bytes 1572880 | tf_op jit(solution)/shard_map/all_gather | solution.py:56
  266.2 6.8 fusion.117
  287.7 88.8 %all-gather.22.cloned.1.call-done = f32[16,2,7,64,64]{4,3,2,1,0:T(8,128)} async-done(((f32[1,2,7,64,64]{4,3,2,1,0:T(8,128)}), f32[16,2,7,64,64]{4,3,2,1,0:T(8,128)}) %all-gather.22.cloned.1.call-update) | async-done | bytes 3670032 | tf_op jit(solution)/shard_map/all_gather | solution.py:60
  395.5 24.4 %fusion.239 = f32[1,64,64,64]{3,2,1,0:T(8,128)S(1)} fusion(f32[1,64,64,64]{3,2,1,0:T(8,128)S(1)} %copy-done.4, f32[1,64,64,7]{3,2,1,0:T(8,128)S(1)} %get-tuple-element.20, f32[1,64,64,64]{3,2,1,0:T(8,128)S(1)} %fusion.117, f32[1,64,64,7]{3,2,1,0:T(8,128)S(1)} %get-tuple-element.19, f32[]{:T(128)} %bitcast.96, f32[]{:T(128)} %bitcast.95, f32[]{:T(128)} %bitcast.94, ...), kind=kLoop, calls=%fused_computation.402 | loop fusion | flops 11534336 | bytes 3375164 | tf_op jit(solution)/shard_map/div | solution.py:119
  426.3 93.2 %all-gather.24.cloned.1.call-done = f32[16,2,7,64,64]{4,3,2,1,0:T(8,128)} async-done(((f32[1,2,7,64,64]{4,3,2,1,0:T(8,128)}), f32[16,2,7,64,64]{4,3,2,1,0:T(8,128)}) %all-gather.24.cloned.1.call-update) | async-done | bytes 3670032 | tf_op jit(solution)/shard_map/all_gather | solution.py:64
  540.2 36.7 %fusion.206 = f32[1,64,64,64]{3,2,1,0:T(8,128)} fusion(f32[1,64,64,7]{3,2,1,0:T(8,128)} %get-tuple-element.18, f32[1,64,64,64]{3,2,1,0:T(8,128)S(1)} %copy-done.3, f32[1,64,64,7]{3,2,1,0:T(8,128)} %get-tuple-element.17, f32[]{:T(128)} %bitcast.96, f32[]{:T(128)} %bitcast.95, f32[]{:T(128)} %bitcast.94, f32[]{:T(128)} %bitcast.93, f32[]{:T(128)} %bitcast.92, ...), kind=kLoop, calls=%fused_computation.343 | loop fusion | flops 11272192 | bytes 2326588 | tf_op jit(solution)/shard_map/add | solution.py:82
  578.8 84.3 %all-gather.26.cloned.1.call-done = f32[16,2,3,64,64]{4,3,2,1,0:T(8,128)} async-done(((f32[1,2,3,64,64]{4,3,2,1,0:T(8,128)}), f32[16,2,3,64,64]{4,3,2,1,0:T(8,128)}) %all-gather.26.cloned.1.call-update) | async-done | bytes 1572880 | tf_op jit(solution)/shard_map/all_gather | solution.py:68
  670.1 7.3 fusion.103
  678.1 84.3 %all-gather.28.cloned.1.call-done = f32[16,2,3,64,64]{4,3,2,1,0:T(8,128)} async-done(((f32[1,2,3,64,64]{4,3,2,1,0:T(8,128)}), f32[16,2,3,64,64]{4,3,2,1,0:T(8,128)}) %all-gather.28.cloned.1.call-update) | async-done | bytes 1572880 | tf_op jit(solution)/shard_map/all_gather | solution.py:68
  768.8 7.4 fusion.47
  776.9 307.0 %all-gather.42.cloned.1.call-done = f32[16,64,64,64]{3,2,1,0:T(8,128)} async-done(((f32[1,64,64,64]{3,2,1,0:T(8,128)}), f32[16,64,64,64]{3,2,1,0:T(8,128)}) %all-gather.42.cloned.1.call-update) | async-done | bytes 16777232 | tf_op jit(solution)/shard_map/all_gather | solution.py:10
  1083.9 14.2 reduce.4
  1102.5 80.1 %all-gather.30.cloned.1.call-done = f32[16,2,3,64,64]{4,3,2,1,0:T(8,128)} async-done(((f32[1,2,3,64,64]{4,3,2,1,0:T(8,128)}), f32[16,2,3,64,64]{4,3,2,1,0:T(8,128)}) %all-gather.30.cloned.1.call-update) | async-done | bytes 1572880 | tf_op jit(solution)/shard_map/all_gather | solution.py:52
  1197.8 84.3 %all-gather.32.cloned.1.call-done = f32[16,2,3,64,64]{4,3,2,1,0:T(8,128)} async-done(((f32[1,2,3,64,64]{4,3,2,1,0:T(8,128)}), f32[16,2,3,64,64]{4,3,2,1,0:T(8,128)}) %all-gather.32.cloned.1.call-update) | async-done | bytes 1572880 | tf_op jit(solution)/shard_map/all_gather | solution.py:56
  1302.2 93.1 %all-gather.34.cloned.1.call-done = f32[16,2,7,64,64]{4,3,2,1,0:T(8,128)} async-done(((f32[1,2,7,64,64]{4,3,2,1,0:T(8,128)}), f32[16,2,7,64,64]{4,3,2,1,0:T(8,128)}) %all-gather.34.cloned.1.call-update) | async-done | bytes 3670032 | tf_op jit(solution)/shard_map/all_gather | solution.py:60
  1414.7 24.4 %fusion.166 = f32[1,64,64,64]{3,2,1,0:T(8,128)S(1)} fusion(f32[1,64,64,64]{3,2,1,0:T(8,128)S(1)} %copy-done.5, f32[1,64,64,7]{3,2,1,0:T(8,128)S(1)} %get-tuple-element.16, f32[1,64,64,64]{3,2,1,0:T(8,128)S(1)} %copy-done.1, f32[1,64,64,7]{3,2,1,0:T(8,128)S(1)} %get-tuple-element.15, f32[]{:T(128)} %bitcast.96, f32[]{:T(128)} %bitcast.95, f32[]{:T(128)} %bitcast.94, ...), kind=kLoop, calls=%fused_computation.269 | loop fusion | flops 11534336 | bytes 3375164 | tf_op jit(solution)/shard_map/div | solution.py:119
  1447.9 92.9 %all-gather.36.cloned.1.call-done = f32[16,2,7,64,64]{4,3,2,1,0:T(8,128)} async-done(((f32[1,2,7,64,64]{4,3,2,1,0:T(8,128)}), f32[16,2,7,64,64]{4,3,2,1,0:T(8,128)}) %all-gather.36.cloned.1.call-update) | async-done | bytes 3670032 | tf_op jit(solution)/shard_map/all_gather | solution.py:64
  1561.3 36.7 %fusion.133 = f32[1,64,64,64]{3,2,1,0:T(8,128)} fusion(f32[1,64,64,7]{3,2,1,0:T(8,128)} %get-tuple-element.14, f32[1,64,64,64]{3,2,1,0:T(8,128)S(1)} %fusion.166, f32[1,64,64,7]{3,2,1,0:T(8,128)} %get-tuple-element.13, f32[]{:T(128)} %bitcast.96, f32[]{:T(128)} %bitcast.95, f32[]{:T(128)} %bitcast.94, f32[]{:T(128)} %bitcast.93, f32[]{:T(128)} %bitcast.92, ...), kind=kLoop, calls=%fused_computation.210 | loop fusion | flops 11272192 | bytes 2326588 | tf_op jit(solution)/shard_map/add | solution.py:82
  1599.9 84.3 %all-gather.38.cloned.1.call-done = f32[16,2,3,64,64]{4,3,2,1,0:T(8,128)} async-done(((f32[1,2,3,64,64]{4,3,2,1,0:T(8,128)}), f32[16,2,3,64,64]{4,3,2,1,0:T(8,128)}) %all-gather.38.cloned.1.call-update) | async-done | bytes 1572880 | tf_op jit(solution)/shard_map/all_gather | solution.py:68
  1691.2 7.1 fusion.75
  1699.0 84.3 %all-gather.40.cloned.1.call-done = f32[16,2,3,64,64]{4,3,2,1,0:T(8,128)} async-done(((f32[1,2,3,64,64]{4,3,2,1,0:T(8,128)}), f32[16,2,3,64,64]{4,3,2,1,0:T(8,128)}) %all-gather.40.cloned.1.call-update) | async-done | bytes 1572880 | tf_op jit(solution)/shard_map/all_gather | solution.py:68
  1798.6 86.1 %reduce-scatter.2.cloned.1.call-done = f32[1,64,4,64]{3,1,0,2:T(8,128)} async-done(((f32[1,64,64,64]{3,1,0,2:T(8,128)}), f32[1,64,4,64]{3,1,0,2:T(8,128)}) %reduce-scatter.2.cloned.1.call-update) | async-done | bytes 65552 | tf_op jit(solution)/shard_map/reduce_scatter | solution.py:128
  (189 shorter events, 224.8 us)
Async XLA Ops:
  6.5 72.1 %copy-start.15 = (f32[1,7]{1,0:T(1,128)S(1)}, f32[1,7]{1,0:T(1,128)}, u32[]{:S(2)}) copy-start(f32[1,7]{1,0:T(1,128)} %param.9) | copy-start | bytes 88
  6.5 72.8 %copy-start.14 = (s32[1,6]{1,0:T(1,128)S(1)}, s32[1,6]{1,0:T(1,128)}, u32[]{:S(2)}) copy-start(s32[1,6]{1,0:T(1,128)} %param.12) | copy-start | bytes 76
  6.5 69.3 %all-gather.16.cloned.1.call-start = ((), (), s32[]{:S(2)}) async-start(), calls=%async_computation.1 | async-start | bytes 2228224 | tf_op jit(solution)/shard_map/all_gather | solution.py:107
  8.2 151.9 %all-gather.18.cloned.1.call-start = ((), (), s32[]{:S(2)}) async-start(), calls=%async_computation.2 | async-start | bytes 3342336 | tf_op jit(solution)/shard_map/all_gather | solution.py:52
  78.6 180.7 %all-gather.20.cloned.1.call-start = ((), (), s32[]{:S(2)}) async-start(), calls=%async_computation.3 | async-start | bytes 3342336 | tf_op jit(solution)/shard_map/all_gather | solution.py:56
  166.4 8.9 copy-start.16
  175.0 201.5 %all-gather.22.cloned.1.call-start = ((), (), s32[]{:S(2)}) async-start(), calls=%async_computation.4 | async-start | bytes 7798784 | tf_op jit(solution)/shard_map/all_gather | solution.py:60
  278.2 5.3 copy-start.17
  278.2 6.0 copy-start.13
  283.1 236.3 %all-gather.24.cloned.1.call-start = ((), (), s32[]{:S(2)}) async-start(), calls=%async_computation.5 | async-start | bytes 7798784 | tf_op jit(solution)/shard_map/all_gather | solution.py:64
  426.1 237.1 %all-gather.26.cloned.1.call-start = ((), (), s32[]{:S(2)}) async-start(), calls=%async_computation.6 | async-start | bytes 3342336 | tf_op jit(solution)/shard_map/all_gather | solution.py:68
  535.2 4.9 copy-start.3
  578.8 183.7 %all-gather.28.cloned.1.call-start = ((), (), s32[]{:S(2)}) async-start(), calls=%async_computation.7 | async-start | bytes 3342336 | tf_op jit(solution)/shard_map/all_gather | solution.py:68
  665.3 4.8 copy-start.8
  678.1 405.8 %all-gather.42.cloned.1.call-start = ((), (), s32[]{:S(2)}) async-start(), calls=%async_computation.15 | async-start | bytes 35651584 | tf_op jit(solution)/shard_map/all_gather | solution.py:10
  776.2 406.4 %all-gather.30.cloned.1.call-start = ((), (), s32[]{:S(2)}) async-start(), calls=%async_computation.8 | async-start | bytes 3342336 | tf_op jit(solution)/shard_map/all_gather | solution.py:52
  1101.6 87.4 %copy-start.6 = (f32[1,64,64,64]{3,2,1,0:T(8,128)}, f32[1,64,64,64]{3,2,1,0:T(8,128)S(1)}, u32[]{:S(2)}) copy-start(f32[1,64,64,64]{3,2,1,0:T(8,128)S(1)} %bitcast_multiply_fusion) | copy-start | bytes 3145732
  1102.5 179.6 %all-gather.32.cloned.1.call-start = ((), (), s32[]{:S(2)}) async-start(), calls=%async_computation.9 | async-start | bytes 3342336 | tf_op jit(solution)/shard_map/all_gather | solution.py:56
  1197.7 197.7 %all-gather.34.cloned.1.call-start = ((), (), s32[]{:S(2)}) async-start(), calls=%async_computation.10 | async-start | bytes 7798784 | tf_op jit(solution)/shard_map/all_gather | solution.py:60
  1284.2 4.8 copy-start.12
  1302.0 238.8 %all-gather.36.cloned.1.call-start = ((), (), s32[]{:S(2)}) async-start(), calls=%async_computation.11 | async-start | bytes 7798784 | tf_op jit(solution)/shard_map/all_gather | solution.py:64
  1447.4 236.9 %all-gather.38.cloned.1.call-start = ((), (), s32[]{:S(2)}) async-start(), calls=%async_computation.12 | async-start | bytes 3342336 | tf_op jit(solution)/shard_map/all_gather | solution.py:68
  1599.9 183.5 %all-gather.40.cloned.1.call-start = ((), (), s32[]{:S(2)}) async-start(), calls=%async_computation.13 | async-start | bytes 3342336 | tf_op jit(solution)/shard_map/all_gather | solution.py:68
  1699.0 185.7 %reduce-scatter.2.cloned.1.call-start = ((), (), s32[]{:S(2)}) async-start(), calls=%async_computation.14 | async-start | bytes 2228224 | tf_op jit(solution)/shard_map/reduce_scatter | solution.py:128
  (9 other events, 25.9 us)
Sparse Core Ops, SparseCore 0:
  10.0 65.7 all-gather.15
  78.7 81.3 all-gather.17
  175.1 84.1 all-gather.19
  283.2 93.2 all-gather.21
  426.2 93.2 all-gather.23
  578.9 84.2 all-gather.25
  678.2 84.1 all-gather.27
  776.3 307.5 all-gather.41
  1102.6 80.0 all-gather.29
  1197.8 84.2 all-gather.31
  1302.1 93.2 all-gather.33
  1447.5 93.2 all-gather.35
  1600.0 84.2 all-gather.37
  1699.1 84.2 all-gather.39
  1798.7 85.9 reduce-scatter.1
